TPU v7x, 256 devices: a whole 4x4x8 slice. The times are simulated.
256 devices in a mesh: seq: 64 (over y, z, core), pb: 4 (over x).
Axes of the slice: x: 4, y: 4, z: 8, core: 2. Of those that a mesh axis runs over, the one named last changes fastest.
Arguments:
- tokens: bfloat16 [16384, 2048], P('seq'), may hold values from -0.119628906 to 0.119628906
- w_query: bfloat16 [2048, 2048], P(None, 'pb')
- w_key: bfloat16 [2048, 2048], P(None, 'pb')
- w_value: bfloat16 [2048, 2048], P(None, 'pb'), may hold values from -0.125 to 0.125
- w_out: bfloat16 [2048, 2048], P('pb'), may hold values from -0.125 to 0.125
- gain_attn: float32 [2048], replicated, may hold values from 0.1 to 1.9
- gain_embed: float32 [2048], replicated, may hold values from 0.1 to 1.9
- queries: bfloat16 [256, 32, 2048], P(('seq', 'pb')), may hold values from -0.125 to 0.125
- query_lengths: int32 [256], P(('seq', 'pb')), may hold values from 8 to 32
- group_lengths: int32 [128], replicated, may hold values from 1 to 1024, 16384 in all
- teacher: float32 [256, 128], P(('seq', 'pb')), may hold values from -12 to 12
Outputs:
- embedded: bfloat16 [16384, 2048], P('seq')
- scores: float32 [256, 128], P(('seq', 'pb'))
- score_gradient: float32 [256, 128], P(('seq', 'pb'))
- distill_loss: float32 [], replicated
Inputs may be any that keep to these rules, and one draw needn't show every extreme that they name: `group_lengths`: the groups cover the document in order: the lengths sum to 16384.
All inputs are finite; a program needn't handle non-finite values.
Results may differ from a plain program's by a relative error of at most 0.013.
Values may be sent and summed in bfloat16 or wider, within the bound.
No kernel may reach another device: no remote copies, remote signals or barrier semaphores. Data moves between devices by JAX's collectives and lax.ppermute only.
A program may use at most 128 MiB of HBM per device.

v0:
```python
import jax
import jax.numpy as jnp
from jax import lax
from jax.sharding import PartitionSpec as P

HD = 128
WIN = 2048
LQ = 32
EPSILON = 1e-06
SOFTMAX_TEMP = 0.1


def shifted_2(x, axis, by):
    count = lax.axis_size(axis)
    pairs = [(i, i + by) for i in range(count) if 0 <= i + by < count]
    return lax.ppermute(x, axis, pairs)


def rms_scale(values, gain):
    mean_sq = jnp.mean(values * values, axis=-1, keepdims=True)
    return values * lax.rsqrt(mean_sq + EPSILON) * gain


def segmented_max(values, group_id):
    span_len = values.shape[-1]
    stride = 1
    while stride < span_len:
        filler = jnp.full(values.shape[:-1] + (stride,), -jnp.inf, values.dtype)
        shifted = jnp.concatenate([filler, values[..., :-stride]], axis=-1)
        prior_id = jnp.concatenate([jnp.full((stride,), -1, jnp.int32), group_id[:-stride]])
        values = jnp.where((prior_id == group_id)[None, :], jnp.maximum(values, shifted), values)
        stride = stride * 2
    return values


def per_device(
    tokens,
    w_query,
    w_key,
    w_value,
    w_out,
    gain_attn,
    gain_embed,
    queries,
    query_lengths,
    group_lengths,
    teacher,
):
    shard_rows = tokens.shape[0]
    seq_count = lax.axis_size("seq")
    seq_place = lax.axis_index("seq")
    head_width = w_query.shape[1]
    heads_here = head_width // HD
    half_win = WIN // 2
    reach_count = half_win // shard_rows
    my_start = seq_place * shard_rows
    total_tokens = shard_rows * seq_count
    residual = tokens.astype(jnp.float32)
    normed = rms_scale(residual, gain_attn).astype(jnp.bfloat16)
    q_local = jnp.dot(normed, w_query, preferred_element_type=jnp.float32).astype(jnp.bfloat16)
    k_local = jnp.dot(normed, w_key, preferred_element_type=jnp.float32).astype(jnp.bfloat16)
    v_local = jnp.dot(normed, w_value, preferred_element_type=jnp.float32).astype(jnp.bfloat16)
    key_value = jnp.stack([k_local, v_local])
    earlier = [shifted_2(key_value, "seq", distance) for distance in range(reach_count, 0, -1)]
    later = [shifted_2(key_value, "seq", -distance) for distance in range(1, reach_count + 1)]
    window = jnp.concatenate(earlier + [key_value] + later, axis=1)
    span_rows = window.shape[1]
    q_pos = my_start + jnp.arange(shard_rows, dtype=jnp.int32)
    k_pos = my_start - reach_count * shard_rows + jnp.arange(span_rows, dtype=jnp.int32)
    in_window = (
        (jnp.abs(q_pos[:, None] - k_pos[None, :]) <= half_win)
        & (k_pos >= 0)[None, :]
        & (k_pos < total_tokens)[None, :]
    )
    q_heads = q_local.reshape(shard_rows, heads_here, HD)
    k_heads = window[0].reshape(span_rows, heads_here, HD)
    v_heads = window[1].reshape(span_rows, heads_here, HD)
    logits = jnp.einsum(
        "qhd,khd->hqk", q_heads, k_heads, preferred_element_type=jnp.float32
    ) * HD ** (-0.5)
    logits = jnp.where(in_window[None], logits, -jnp.inf)
    row_max = jnp.max(logits, axis=-1, keepdims=True)
    exp_terms = jnp.exp(logits - row_max)
    weights = (exp_terms / jnp.sum(exp_terms, axis=-1, keepdims=True)).astype(jnp.bfloat16)
    mixed = jnp.einsum("hqk,khd->qhd", weights, v_heads, preferred_element_type=jnp.float32)
    mixed = mixed.reshape(shard_rows, head_width).astype(jnp.bfloat16)
    partial_value = jnp.dot(mixed, w_out, preferred_element_type=jnp.float32)
    attn_sum = lax.psum(partial_value, "pb")
    embedded = rms_scale(residual + attn_sum, gain_embed).astype(jnp.bfloat16)
    group_end = jnp.cumsum(group_lengths)
    group_start = group_end - group_lengths
    group_id = jnp.sum((group_end[None, :] <= q_pos[:, None]).astype(jnp.int32), axis=1)
    last_local = jnp.clip(group_end - 1 - my_start, 0, shard_rows - 1)
    present = (group_start < my_start + shard_rows) & (group_end > my_start)
    q_piece = lax.all_gather(queries, "seq", axis=0, tiled=True)
    count = q_piece.shape[0]
    q_rows = q_piece.reshape(count * q_piece.shape[1], q_piece.shape[2])
    similar = jnp.einsum("td,rd->tr", q_rows, embedded, preferred_element_type=jnp.float32)
    running = segmented_max(similar, group_id)
    picked = jnp.take(running, last_local, axis=1)
    picked = jnp.where(present[None, :], picked, -jnp.inf)
    part_max = picked.reshape(count, q_piece.shape[1], picked.shape[-1])
    own_count = queries.shape[0]
    all_maxima = lax.pmax(part_max, "seq")
    token_max = lax.dynamic_slice_in_dim(all_maxima, seq_place * own_count, own_count, 0)
    live_mask = (jnp.arange(LQ, dtype=jnp.int32)[None, :] < query_lengths[:, None]).astype(
        jnp.float32
    )
    scores = (
        jnp.sum(token_max * live_mask[:, :, None], axis=1)
        / query_lengths.astype(jnp.float32)[:, None]
    )
    student_scores = scores / SOFTMAX_TEMP
    student_scores = student_scores - jnp.max(student_scores, axis=-1, keepdims=True)
    student_log_prob = student_scores - jnp.log(
        jnp.sum(jnp.exp(student_scores), axis=-1, keepdims=True)
    )
    target_scores = teacher / SOFTMAX_TEMP
    target_scores = target_scores - jnp.max(target_scores, axis=-1, keepdims=True)
    log_t = target_scores - jnp.log(jnp.sum(jnp.exp(target_scores), axis=-1, keepdims=True))
    teacher_prob = jnp.exp(log_t)
    kl_terms = jnp.sum(teacher_prob * (log_t - student_log_prob), axis=-1)
    query_count_all = own_count * seq_count * lax.axis_size("pb")
    distill_loss = lax.psum(jnp.sum(kl_terms), ("seq", "pb")) / query_count_all
    score_gradient = (jnp.exp(student_log_prob) - teacher_prob) / (SOFTMAX_TEMP * query_count_all)
    return (embedded, scores, score_gradient, distill_loss)


def solution(mesh):
    placed = (
        P("seq", None),
        P(None, "pb"),
        P(None, "pb"),
        P(None, "pb"),
        P("pb", None),
        P(),
        P(),
        P(("seq", "pb"), None, None),
        P(("seq", "pb")),
        P(),
        P(("seq", "pb"), None),
    )
    return jax.shard_map(
        per_device,
        mesh=mesh,
        in_specs=placed,
        out_specs=(P("seq", None), P(("seq", "pb"), None), P(("seq", "pb"), None), P()),
        check_vma=False,
    )
```

profile of v0, /device:TPU:1, one launch (start us, length us, event | category | flops | bytes accessed | tf_op | source)
XLA Modules:
  0.0 512.5 jit_solution(6274992664846566963)
XLA Ops:
  8.1 1.6 fusion.10
  9.8 2.8 fusion.15
  12.6 0.7 fusion.14
  13.4 0.7 copy-done.5
  14.1 0.8 pad_maximum_fusion
  14.9 6.5 %collective-permute-start = (bf16[2,256,512]{2,1,0:T(8,128)(2,1)}, bf16[2,256,512]{2,1,0:T(8,128)(2,1)}, u32[]{:S(2)}, u32[]{:S(2)}) collective-permute-start(bf16[2,256,512]{2,1,0:T(8,128)(2,1)} %pad_maximum_fusion), channel_id=1, source_target_pairs={{0,16},{4,20},{8,24},{12,28},{16,32},{20,36},{24,40},{28,44},{32,4... | collective-permute-start | bytes 1572872 | tf_op jit(solution)/shard_map/ppermute | solution.py:16
  21.5 7.0 %collective-permute-start.1 = (bf16[2,256,512]{2,1,0:T(8,128)(2,1)}, bf16[2,256,512]{2,1,0:T(8,128)(2,1)}, u32[]{:S(2)}, u32[]{:S(2)}) collective-permute-start(bf16[2,256,512]{2,1,0:T(8,128)(2,1)} %pad_maximum_fusion), channel_id=1, source_target_pairs={{0,12},{4,16},{8,20},{12,24},{16,28},{20,32},{24,36},{28,40},{32,4... | collective-permute-start | bytes 1572872 | tf_op jit(solution)/shard_map/ppermute | solution.py:16
  28.4 2.6 collective-permute-start.2
  31.1 1.9 collective-permute-start.3
  33.0 3.2 collective-permute-start.4
  36.3 1.7 fusion.9
  37.9 3.0 fusion.16
  41.0 1.4 collective-permute-start.5
  42.4 1.1 constant_dynamic-update-slice_fusion.8
  43.5 14.3 %collective-permute-done.1 = bf16[2,256,512]{2,1,0:T(8,128)(2,1)} collective-permute-done((bf16[2,256,512]{2,1,0:T(8,128)(2,1)}, bf16[2,256,512]{2,1,0:T(8,128)(2,1)}, u32[]{:S(2)}, u32[]{:S(2)}) %collective-permute-start.1) | collective-permute-done | bytes 524320 | tf_op jit(solution)/shard_map/ppermute | solution.py:16
  57.7 1.3 collective-permute-start.6
  59.0 1.1 constant_dynamic-update-slice_fusion.7
  60.1 10.9 %collective-permute-done.2 = bf16[2,256,512]{2,1,0:T(8,128)(2,1)} collective-permute-done((bf16[2,256,512]{2,1,0:T(8,128)(2,1)}, bf16[2,256,512]{2,1,0:T(8,128)(2,1)}, u32[]{:S(2)}, u32[]{:S(2)}) %collective-permute-start.2) | collective-permute-done | bytes 524320 | tf_op jit(solution)/shard_map/ppermute | solution.py:16
  71.0 1.3 collective-permute-start.7
  72.2 1.1 constant_dynamic-update-slice_fusion.6
  73.3 4.4 collective-permute-done.3
  77.7 1.1 constant_dynamic-update-slice_fusion.5
  78.9 1.1 constant_dynamic-update-slice_fusion.3
  80.0 17.2 %collective-permute-done.6 = bf16[2,256,512]{2,1,0:T(8,128)(2,1)S(1)} collective-permute-done((bf16[2,256,512]{2,1,0:T(8,128)(2,1)}, bf16[2,256,512]{2,1,0:T(8,128)(2,1)S(1)}, u32[]{:S(2)}, u32[]{:S(2)}) %collective-permute-start.6) | collective-permute-done | bytes 524320 | tf_op jit(solution)/shard_map/ppermute | solution.py:16
  97.2 8.1 %collective-permute-done.7 = bf16[2,256,512]{2,1,0:T(8,128)(2,1)S(1)} collective-permute-done((bf16[2,256,512]{2,1,0:T(8,128)(2,1)}, bf16[2,256,512]{2,1,0:T(8,128)(2,1)S(1)}, u32[]{:S(2)}, u32[]{:S(2)}) %collective-permute-start.7) | collective-permute-done | bytes 524320 | tf_op jit(solution)/shard_map/ppermute | solution.py:16
  105.4 2.4 fusion.39
  107.8 4.3 copy.34
  112.1 5.3 %reshape_squeeze.7 = bf16[2304,4,128]{2,1,0:T(4,128)(2,1)} reshape(bf16[1,2304,512]{2,1,0:T(8,128)(2,1)} %get-tuple-element.8) | data formatting | bytes 4718592 | tf_op jit(solution)/shard_map/reshape;squeeze | solution.py:76
  117.4 8.8 %fusion.40 = (f32[4,256]{1,0:T(4,128)S(1)}, f32[4,256,2304]{2,1,0:T(8,128)}) fusion(pred[256,2304]{1,0:T(8,128)(4,1)} %fusion.9, bf16[2304,4,128]{2,1,0:T(4,128)(2,1)} %reshape_squeeze.7, bf16[32,4,8,128]{3,2,1,0:T(8,128)(2,1)S(1)} %copy-done.13), kind=kOutput, calls=%fused_computation.89 | convolution fusion | flops 613419264 | bytes 12652544 | tf_op jit(solution)/shard_map/sub | solution.py:83
  126.2 6.2 %fusion.13 = bf16[4,128,256]{2,1,0:T(8,128)(2,1)S(1)} fusion(bf16[2304,4,128]{0,2,1:T(8,128)(2,1)} %bitcast.54, f32[4,256,2304]{2,1,0:T(8,128)} %get-tuple-element.23, f32[4,256]{1,0:T(4,128)S(1)} %get-tuple-element.22), kind=kOutput, calls=%fused_computation.32 | convolution fusion | flops 608829440 | bytes 12062720 | tf_op jit(solution)/shard_map/hqk,khd->qhd/dot_general | solution.py:85
  132.4 2.0 fusion.45
  134.5 0.5 all-gather.2.cloned.1.call-update
  135.0 0.2 all-reduce.20.cloned.1.call-start
  135.3 0.1 copy.32
  135.4 0.2 reduce-window.4
  135.7 0.2 convert_reduce_fusion
  136.0 66.0 %all-reduce.18.cloned.1.call-done = f32[256,2048]{1,0:T(8,128)} async-done(((f32[256,2048]{1,0:T(8,128)}), f32[256,2048]{1,0:T(8,128)}) %all-reduce.18.cloned.1.call-update) | async-done | bytes 2097168 | tf_op jit(solution)/shard_map/psum | solution.py:88
  202.0 2.1 multiply_reduce_fusion
  204.3 0.4 multiply_convert_fusion
  204.7 20.3 %all-gather.2.cloned.1.call-done = bf16[64,32,2048]{2,1,0:T(8,128)(2,1)} async-done(((bf16[1,32,2048]{2,1,0:T(8,128)(2,1)}), bf16[64,32,2048]{2,1,0:T(8,128)(2,1)}) %all-gather.2.cloned.1.call-update) | async-done | bytes 8388624 | tf_op jit(solution)/shard_map/all_gather | solution.py:95
  225.0 5.7 %convolution_bitcast_fusion = f32[2048,256]{0,1:T(8,128)S(1)} fusion(bf16[256,2048]{1,0:T(8,128)(2,1)S(1)} %multiply_convert_fusion, bf16[2048,2048]{1,0:T(8,128)(2,1)} %bitcast.65), kind=kOutput, calls=%fused_computation.21 | convolution fusion | flops 2147483648 | bytes 11534336 | tf_op jit(solution)/shard_map/td,rd->tr/dot_general | solution.py:98
  230.7 0.3 maximum_select_fusion.7
  231.1 0.4 maximum_select_fusion.6
  231.4 0.4 maximum_select_fusion.5
  231.8 0.2 slice.79
  232.0 0.3 maximum_select_fusion.4
  232.3 0.2 slice.80
  232.5 0.3 maximum_select_fusion.3
  232.8 0.2 slice.81
  233.0 0.3 maximum_select_fusion.2
  233.4 0.1 slice.82
  233.5 0.3 maximum_select_fusion.1
  233.9 0.3 maximum_select_fusion
  234.2 1.0 gather_fusion
  235.2 1.4 copy.33
  236.6 2.4 select_select_fusion
  239.6 0.6 multiply_reduce_fusion.3
  240.3 1.2 exponential_reduce_fusion
  242.2 178.2 %all-reduce.20.cloned.1.call-done = f32[64,32,128]{2,1,0:T(8,128)} async-done(((f32[64,32,128]{2,1,0:T(8,128)}), f32[64,32,128]{2,1,0:T(8,128)}) %all-reduce.20.cloned.1.call-update) | async-done | bytes 1048592 | tf_op jit(solution)/shard_map/pmax | solution.py:104
  420.3 0.8 multiply_reduce_fusion.1
  421.2 0.6 multiply_reduce_fusion.4
  421.8 1.3 exponential_reduce_fusion.1
  423.7 2.5 multiply_reduce_fusion.2
  426.2 77.1 %psum.15 = f32[]{:T(128)} all-reduce(f32[]{:T(128)} %get-tuple-element.10), channel_id=1, replica_groups=mesh['seq'=64,'pb'=4] {'seq','pb'}, use_global_device_ids=true, to_apply=%region_14.15 | all-reduce | flops 1 | bytes 8 | tf_op jit(solution)/shard_map/psum | solution.py:124
  (50 shorter events, 0.8 us)
Async XLA Ops:
  8.0 124.4 %copy-start = (bf16[512,2048]{1,0:T(8,128)(2,1)S(1)}, bf16[512,2048]{1,0:T(8,128)(2,1)}, u32[]{:S(2)}) copy-start(bf16[512,2048]{1,0:T(8,128)(2,1)} %param.15) | copy-start | bytes 6291460
  8.0 194.0 %all-reduce.18.cloned.1.call-start = ((), (), s32[]{:S(2)}) async-start(), calls=%async_computation | async-start | bytes 4194304 | tf_op jit(solution)/shard_map/psum | solution.py:88
  9.7 2.9 copy-start.2
  9.7 2.9 copy-start.11
  9.7 2.9 copy-start.12
  13.4 0.7 copy-start.5
  14.9 26.0 %collective-permute-start = (bf16[2,256,512]{2,1,0:T(8,128)(2,1)}, bf16[2,256,512]{2,1,0:T(8,128)(2,1)}, u32[]{:S(2)}, u32[]{:S(2)}) collective-permute-start(bf16[2,256,512]{2,1,0:T(8,128)(2,1)} %pad_maximum_fusion), channel_id=1, source_target_pairs={{0,16},{4,20},{8,24},{12,28},{16,32},{20,36},{24,40},{28,44},{32,4... | collective-permute-start | bytes 1572872 | tf_op jit(solution)/shard_map/ppermute | solution.py:16
  21.5 36.2 %collective-permute-start.1 = (bf16[2,256,512]{2,1,0:T(8,128)(2,1)}, bf16[2,256,512]{2,1,0:T(8,128)(2,1)}, u32[]{:S(2)}, u32[]{:S(2)}) collective-permute-start(bf16[2,256,512]{2,1,0:T(8,128)(2,1)} %pad_maximum_fusion), channel_id=1, source_target_pairs={{0,12},{4,16},{8,20},{12,24},{16,28},{20,32},{24,36},{28,40},{32,4... | collective-permute-start | bytes 1572872 | tf_op jit(solution)/shard_map/ppermute | solution.py:16
  28.4 42.5 %collective-permute-start.2 = (bf16[2,256,512]{2,1,0:T(8,128)(2,1)}, bf16[2,256,512]{2,1,0:T(8,128)(2,1)}, u32[]{:S(2)}, u32[]{:S(2)}) collective-permute-start(bf16[2,256,512]{2,1,0:T(8,128)(2,1)} %pad_maximum_fusion), channel_id=1, source_target_pairs={{0,8},{4,12},{8,16},{12,20},{16,24},{20,28},{24,32},{28,36},{32,40... | collective-permute-start | bytes 1572872 | tf_op jit(solution)/shard_map/ppermute | solution.py:16
  31.1 46.6 %collective-permute-start.3 = (bf16[2,256,512]{2,1,0:T(8,128)(2,1)}, bf16[2,256,512]{2,1,0:T(8,128)(2,1)}, u32[]{:S(2)}, u32[]{:S(2)}) collective-permute-start(bf16[2,256,512]{2,1,0:T(8,128)(2,1)} %pad_maximum_fusion), channel_id=1, source_target_pairs={{0,4},{4,8},{8,12},{12,16},{16,20},{20,24},{24,28},{28,32},{32,36}... | collective-permute-start | bytes 1572872 | tf_op jit(solution)/shard_map/ppermute | solution.py:16
  33.0 45.9 %collective-permute-start.4 = (bf16[2,256,512]{2,1,0:T(8,128)(2,1)}, bf16[2,256,512]{2,1,0:T(8,128)(2,1)}, u32[]{:S(2)}, u32[]{:S(2)}) collective-permute-start(bf16[2,256,512]{2,1,0:T(8,128)(2,1)} %pad_maximum_fusion), channel_id=1, source_target_pairs={{4,0},{8,4},{12,8},{16,12},{20,16},{24,20},{28,24},{32,28},{36,32}... | collective-permute-start | bytes 1572872 | tf_op jit(solution)/shard_map/ppermute | solution.py:16
  41.0 37.8 %copy-start.6 = (bf16[1,256,512]{2,1,0:T(8,128)(2,1)S(1)}, bf16[1,256,512]{2,1,0:T(8,128)(2,1)}, u32[]{:S(2)}) copy-start(bf16[1,256,512]{2,1,0:T(8,128)(2,1)} %copy-done.5) | copy-start | bytes 786436
  41.0 39.0 %collective-permute-start.5 = (bf16[2,256,512]{2,1,0:T(8,128)(2,1)}, bf16[2,256,512]{2,1,0:T(8,128)(2,1)S(1)}, u32[]{:S(2)}, u32[]{:S(2)}) collective-permute-start(bf16[2,256,512]{2,1,0:T(8,128)(2,1)} %pad_maximum_fusion), channel_id=1, source_target_pairs={{8,0},{12,4},{16,8},{20,12},{24,16},{28,20},{32,24},{36,28},{40,32... | collective-permute-start | bytes 1572872 | tf_op jit(solution)/shard_map/ppermute | solution.py:16
  57.7 39.4 %collective-permute-start.6 = (bf16[2,256,512]{2,1,0:T(8,128)(2,1)}, bf16[2,256,512]{2,1,0:T(8,128)(2,1)S(1)}, u32[]{:S(2)}, u32[]{:S(2)}) collective-permute-start(bf16[2,256,512]{2,1,0:T(8,128)(2,1)} %pad_maximum_fusion), channel_id=1, source_target_pairs={{12,0},{16,4},{20,8},{24,12},{28,16},{32,20},{36,24},{40,28},{44,3... | collective-permute-start | bytes 1572872 | tf_op jit(solution)/shard_map/ppermute | solution.py:16
  71.0 34.4 %collective-permute-start.7 = (bf16[2,256,512]{2,1,0:T(8,128)(2,1)}, bf16[2,256,512]{2,1,0:T(8,128)(2,1)S(1)}, u32[]{:S(2)}, u32[]{:S(2)}) collective-permute-start(bf16[2,256,512]{2,1,0:T(8,128)(2,1)} %pad_maximum_fusion), channel_id=1, source_target_pairs={{16,0},{20,4},{24,8},{28,12},{32,16},{36,20},{40,24},{44,28},{48,3... | collective-permute-start | bytes 1572872 | tf_op jit(solution)/shard_map/ppermute | solution.py:16
  112.1 5.3 %copy-start.13 = (bf16[32,4,8,128]{3,2,1,0:T(8,128)(2,1)S(1)}, bf16[32,4,8,128]{3,2,1,0:T(8,128)(2,1)}, u32[]{:S(2)}) copy-start(bf16[32,4,8,128]{3,2,1,0:T(8,128)(2,1)} %fusion.16) | copy-start | bytes 786436
  134.4 0.8 copy-start.8
  134.4 69.7 %copy-start.7 = (f32[2048]{0:T(1024)S(1)}, f32[2048]{0:T(1024)}, u32[]{:S(2)}) copy-start(f32[2048]{0:T(1024)} %param.17) | copy-start | bytes 24580
  134.5 90.5 %all-gather.2.cloned.1.call-start = ((), (), s32[]{:S(2)}) async-start(), calls=%async_computation.1 | async-start | bytes 8519680 | tf_op jit(solution)/shard_map/all_gather | solution.py:95
  135.0 285.3 %all-reduce.20.cloned.1.call-start = ((), (), s32[]{:S(2)}) async-start(), calls=%async_computation.2 | async-start | bytes 2097152 | tf_op jit(solution)/shard_map/pmax | solution.py:104
  202.0 2.3 copy-start.3
  204.6 26.1 %copy-start.4 = (bf16[256,2048]{1,0:T(8,128)(2,1)}, bf16[256,2048]{1,0:T(8,128)(2,1)S(1)}, u32[]{:S(2)}) copy-start(bf16[256,2048]{1,0:T(8,128)(2,1)S(1)} %multiply_convert_fusion) | copy-start | bytes 3145732
  235.2 268.7 %copy-start.1 = (bf16[512,2048]{1,0:T(8,128)(2,1)S(1)}, bf16[512,2048]{1,0:T(8,128)(2,1)}, u32[]{:S(2)}) copy-start(bf16[512,2048]{1,0:T(8,128)(2,1)} %param.15) | copy-start | bytes 6291460
  236.6 3.0 copy-start.10
  421.8 82.2 %copy-start.9 = (f32[128]{0:T(128)}, f32[128]{0:T(128)S(1)}, u32[]{:S(2)}) copy-start(f32[128]{0:T(128)S(1)} %get-tuple-element.7) | copy-start | bytes 1540
Sparse Core Ops, SparseCore 0:
  134.6 67.3 all-reduce.17
Sparse Core Ops, SparseCore 1:
  137.7 87.2 all-gather.1
  239.1 181.2 all-reduce.19
where the time goes:
time: 514 us; the launch traced here: 513 us
  waiting for transfers between devices  320 us (62%)
  blocking collectives  77.1 us (15%)
  matrix products  29.3 us (6%)
  starting transfers between devices  25.5 us (5%)
  local copies, waits for them, and re-layouts  21.7 us (4%)
  between operations  19.7 us (4%)
  other arithmetic  19.2 us (4%)
    pmax x1, waiting for transfers between devices, per_device(): all_maxima = lax.pmax(part_max, 'seq')  178 us
    psum x1, blocking collectives, per_device(): distill_loss = lax.psum(jnp.sum(kl_terms), ('seq', 'pb')) / query_count_all  77.1 us
    psum x1, waiting for transfers between devices, per_device(): attn_sum = lax.psum(partial_value, 'pb')  66 us
    ppermute x8, waiting for transfers between devices, shifted_2(): return lax.ppermute(x, axis, pairs)  54.8 us
    ppermute x8, starting transfers between devices, shifted_2(): return lax.ppermute(x, axis, pairs)  25.2 us
    all_gather x1, waiting for transfers between devices, per_device(): q_piece = lax.all_gather(queries, 'seq', axis=0, tiled=True)  20.3 us
  transfers between devices with their start and end apart: 11, of which 8 were waited for; matrix products, arithmetic and copies ran while one was open for 3% of the time, Pallas kernels for 0%

commit v1 on v0

--- a/solution.py
+++ b/solution.py
@@ -92,7 +92,15 @@
     group_id = jnp.sum((group_end[None, :] <= q_pos[:, None]).astype(jnp.int32), axis=1)
     last_local = jnp.clip(group_end - 1 - my_start, 0, shard_rows - 1)
     present = (group_start < my_start + shard_rows) & (group_end > my_start)
-    q_piece = lax.all_gather(queries, "seq", axis=0, tiled=True)
+    q_piece = jnp.concatenate(
+        lax.all_to_all(
+            jnp.stack([queries for _ in range(lax.psum(1, "seq"))]),
+            "seq",
+            split_axis=0,
+            concat_axis=0,
+        ),
+        axis=0,
+    )
     count = q_piece.shape[0]
     q_rows = q_piece.reshape(count * q_piece.shape[1], q_piece.shape[2])
     similar = jnp.einsum("td,rd->tr", q_rows, embedded, preferred_element_type=jnp.float32)

time: 514 us -> 682 us (1.33)
  waiting for transfers between devices: 320 us -> 474 us
  starting transfers between devices: 25.5 us -> 35.8 us
    ppermute x8, waiting for transfers between devices: 54.8 us -> 227 us  [shifted_2(): return lax.ppermute(x, axis, pairs)]
    all_gather x1 -> x0, waiting for transfers between devices: 20.3 us -> none  [per_device(): q_piece = lax.all_gather(queries, 'seq', axis=0, tiled=True)]
    all_to_all x0 -> x1, starting transfers between devices: none -> 13.5 us  [per_device(): lax.all_to_all(jnp.stack([queries for _ in range(lax.psum(1, 'seq'))]), '...]
  transfers between devices with their start and end apart: 11 -> 11, of which waited for: 8 -> 8; matrix products, arithmetic and copies ran while one was open for 3% -> 7% of each run, Pallas kernels for 0% -> 0%
where the time goes in v1:
time: 682 us; the launch traced here: 681 us
  waiting for transfers between devices  474 us (70%)
  blocking collectives  77.2 us (11%)
  starting transfers between devices  35.8 us (5%)
  matrix products  29.3 us (4%)
  local copies, waits for them, and re-layouts  27.3 us (4%)
  other arithmetic  18.8 us (3%)
  between operations  18.3 us (3%)
    ppermute x8, waiting for transfers between devices, shifted_2(): return lax.ppermute(x, axis, pairs)  227 us
    pmax x1, waiting for transfers between devices, per_device(): all_maxima = lax.pmax(part_max, 'seq')  182 us
    psum x1, blocking collectives, per_device(): distill_loss = lax.psum(jnp.sum(kl_terms), ('seq', 'pb')) / query_count_all  77.2 us
    psum x1, waiting for transfers between devices, per_device(): attn_sum = lax.psum(partial_value, 'pb')  64.8 us
    ppermute x8, starting transfers between devices, shifted_2(): return lax.ppermute(x, axis, pairs)  22 us
  transfers between devices with their start and end apart: 11, of which 8 were waited for; matrix products, arithmetic and copies ran while one was open for 7% of the time, Pallas kernels for 0%

profile of v1, /device:TPU:1, one launch (start us, length us, event | category | flops | bytes accessed | tf_op | source)
XLA Modules:
  0.0 681.0 jit_solution(9934922077729418531)
XLA Ops:
  7.2 5.4 stack.11
  12.6 13.5 %all-to-all-start = ((bf16[64,1,32,2048]{3,2,1,0:T(8,128)(2,1)}), bf16[64,1,32,2048]{3,2,1,0:T(8,128)(2,1)}, u32[]{:S(2)}, u32[]{:S(2)}) async-start(bf16[64,1,32,2048]{3,2,1,0:T(8,128)(2,1)} %stack.11), calls=%async_computation | async-start | bytes 16777216 | tf_op jit(solution)/shard_map/all_to_all | solution.py:96
  26.1 0.3 fusion.10
  26.5 2.5 fusion.14
  29.0 0.8 fusion.15
  29.7 0.7 copy-done.4
  30.5 0.8 pad_maximum_fusion
  31.3 5.0 collective-permute-start
  36.3 5.8 collective-permute-start.1
  42.0 2.2 collective-permute-start.2
  44.2 1.9 collective-permute-start.3
  46.1 3.2 collective-permute-start.4
  49.4 1.7 fusion.9
  51.0 3.1 fusion.16
  54.1 174.2 %collective-permute-done = bf16[2,256,512]{2,1,0:T(8,128)(2,1)} collective-permute-done((bf16[2,256,512]{2,1,0:T(8,128)(2,1)}, bf16[2,256,512]{2,1,0:T(8,128)(2,1)}, u32[]{:S(2)}, u32[]{:S(2)}) %collective-permute-start) | collective-permute-done | bytes 524320 | tf_op jit(solution)/shard_map/ppermute | solution.py:16
  228.3 1.3 collective-permute-start.5
  229.6 1.1 constant_dynamic-update-slice_fusion.8
  230.7 13.6 %collective-permute-done.1 = bf16[2,256,512]{2,1,0:T(8,128)(2,1)} collective-permute-done((bf16[2,256,512]{2,1,0:T(8,128)(2,1)}, bf16[2,256,512]{2,1,0:T(8,128)(2,1)}, u32[]{:S(2)}, u32[]{:S(2)}) %collective-permute-start.1) | collective-permute-done | bytes 524320 | tf_op jit(solution)/shard_map/ppermute | solution.py:16
  244.3 1.3 collective-permute-start.6
  245.6 1.1 constant_dynamic-update-slice_fusion.7
  246.7 9.9 %collective-permute-done.2 = bf16[2,256,512]{2,1,0:T(8,128)(2,1)} collective-permute-done((bf16[2,256,512]{2,1,0:T(8,128)(2,1)}, bf16[2,256,512]{2,1,0:T(8,128)(2,1)}, u32[]{:S(2)}, u32[]{:S(2)}) %collective-permute-start.2) | collective-permute-done | bytes 524320 | tf_op jit(solution)/shard_map/ppermute | solution.py:16
  256.6 1.5 collective-permute-start.7
  258.0 1.1 constant_dynamic-update-slice_fusion.6
  259.1 3.6 collective-permute-done.3
  262.7 1.1 constant_dynamic-update-slice_fusion.5
  263.8 1.1 constant_dynamic-update-slice_fusion.3
  265.0 3.8 collective-permute-done.6
  268.8 22.1 %collective-permute-done.7 = bf16[2,256,512]{2,1,0:T(8,128)(2,1)S(1)} collective-permute-done((bf16[2,256,512]{2,1,0:T(8,128)(2,1)}, bf16[2,256,512]{2,1,0:T(8,128)(2,1)S(1)}, u32[]{:S(2)}, u32[]{:S(2)}) %collective-permute-start.7) | collective-permute-done | bytes 524320 | tf_op jit(solution)/shard_map/ppermute | solution.py:16
  291.0 2.4 fusion.39
  293.4 5.3 reshape_squeeze.7
  298.7 4.4 copy.29
  303.0 8.8 %fusion.40 = (f32[4,256]{1,0:T(4,128)S(1)}, f32[4,256,2304]{2,1,0:T(8,128)}) fusion(pred[256,2304]{1,0:T(8,128)(4,1)} %fusion.9, bf16[2304,4,128]{2,1,0:T(4,128)(2,1)} %reshape_squeeze.7, bf16[32,4,8,128]{3,2,1,0:T(8,128)(2,1)S(1)} %copy-done.12), kind=kOutput, calls=%fused_computation.89 | convolution fusion | flops 613419264 | bytes 12652544 | tf_op jit(solution)/shard_map/sub | solution.py:83
  311.8 6.2 fusion.13
  318.0 2.0 fusion.45
  320.1 0.3 all-reduce.20.cloned.1.call-start
  320.3 0.3 copy-done.7
  320.8 0.2 reduce-window.4
  321.1 0.2 convert_reduce_fusion
  321.4 64.8 %all-reduce.18.cloned.1.call-done = f32[256,2048]{1,0:T(8,128)} async-done(((f32[256,2048]{1,0:T(8,128)}), f32[256,2048]{1,0:T(8,128)}) %all-reduce.18.cloned.1.call-update) | async-done | bytes 2097168 | tf_op jit(solution)/shard_map/psum | solution.py:88
  386.2 2.1 multiply_reduce_fusion
  388.4 1.3 multiply_convert_fusion
  389.7 6.1 convolution_bitcast_fusion
  395.8 0.3 maximum_select_fusion.7
  396.1 0.3 maximum_select_fusion.6
  396.5 0.4 maximum_select_fusion.5
  396.8 0.1 slice.79
  397.0 0.3 maximum_select_fusion.4
  397.3 0.2 slice.80
  397.5 0.3 maximum_select_fusion.3
  397.8 0.1 slice.81
  397.9 0.3 maximum_select_fusion.2
  398.3 0.4 maximum_select_fusion.1
  398.8 0.3 maximum_select_fusion
  399.1 1.0 gather_fusion
  400.1 1.4 copy.28
  401.5 2.4 select_select_fusion
  404.5 0.6 multiply_reduce_fusion.3
  405.2 1.2 exponential_reduce_fusion
  407.1 182.3 %all-reduce.20.cloned.1.call-done = f32[64,32,128]{2,1,0:T(8,128)} async-done(((f32[64,32,128]{2,1,0:T(8,128)}), f32[64,32,128]{2,1,0:T(8,128)}) %all-reduce.20.cloned.1.call-update) | async-done | bytes 1048592 | tf_op jit(solution)/shard_map/pmax | solution.py:112
  589.4 0.8 multiply_reduce_fusion.1
  590.2 0.6 multiply_reduce_fusion.4
  590.8 1.3 exponential_reduce_fusion.1
  592.7 2.5 multiply_reduce_fusion.2
  595.2 77.2 %psum.15 = f32[]{:T(128)} all-reduce(f32[]{:T(128)} %get-tuple-element.10), channel_id=1, replica_groups=mesh['seq'=64,'pb'=4] {'seq','pb'}, use_global_device_ids=true, to_apply=%region_14.15 | all-reduce | flops 1 | bytes 8 | tf_op jit(solution)/shard_map/psum | solution.py:132
  (48 shorter events, 1.0 us)
Async XLA Ops:
  7.2 310.8 %copy-start = (bf16[512,2048]{1,0:T(8,128)(2,1)S(1)}, bf16[512,2048]{1,0:T(8,128)(2,1)}, u32[]{:S(2)}) copy-start(bf16[512,2048]{1,0:T(8,128)(2,1)} %param.15) | copy-start | bytes 6291460
  12.6 13.5 %copy-start.2 = (bf16[256,2048]{1,0:T(8,128)(2,1)S(1)}, bf16[256,2048]{1,0:T(8,128)(2,1)}, u32[]{:S(2)}) copy-start(bf16[256,2048]{1,0:T(8,128)(2,1)} %param.11) | copy-start | bytes 3145732
  12.6 13.8 %copy-start.11 = (f32[2048]{0:T(1024)S(1)}, f32[2048]{0:T(1024)}, u32[]{:S(2)}) copy-start(f32[2048]{0:T(1024)} %param.16) | copy-start | bytes 24580
  12.6 377.1 %all-to-all-start = ((bf16[64,1,32,2048]{3,2,1,0:T(8,128)(2,1)}), bf16[64,1,32,2048]{3,2,1,0:T(8,128)(2,1)}, u32[]{:S(2)}, u32[]{:S(2)}) async-start(bf16[64,1,32,2048]{3,2,1,0:T(8,128)(2,1)} %stack.11), calls=%async_computation | async-start | bytes 16777216 | tf_op jit(solution)/shard_map/all_to_all | solution.py:96
  26.1 360.1 %all-reduce.18.cloned.1.call-start = ((), (), s32[]{:S(2)}) async-start(), calls=%async_computation.1 | async-start | bytes 4194304 | tf_op jit(solution)/shard_map/psum | solution.py:88
  26.4 2.5 copy-start.10
  29.7 0.7 copy-start.4
  31.3 197.1 %collective-permute-start = (bf16[2,256,512]{2,1,0:T(8,128)(2,1)}, bf16[2,256,512]{2,1,0:T(8,128)(2,1)}, u32[]{:S(2)}, u32[]{:S(2)}) collective-permute-start(bf16[2,256,512]{2,1,0:T(8,128)(2,1)} %pad_maximum_fusion), channel_id=1, source_target_pairs={{0,16},{4,20},{8,24},{12,28},{16,32},{20,36},{24,40},{28,44},{32,4... | collective-permute-start | bytes 1572872 | tf_op jit(solution)/shard_map/ppermute | solution.py:16
  36.3 208.0 %collective-permute-start.1 = (bf16[2,256,512]{2,1,0:T(8,128)(2,1)}, bf16[2,256,512]{2,1,0:T(8,128)(2,1)}, u32[]{:S(2)}, u32[]{:S(2)}) collective-permute-start(bf16[2,256,512]{2,1,0:T(8,128)(2,1)} %pad_maximum_fusion), channel_id=1, source_target_pairs={{0,12},{4,16},{8,20},{12,24},{16,28},{20,32},{24,36},{28,40},{32,4... | collective-permute-start | bytes 1572872 | tf_op jit(solution)/shard_map/ppermute | solution.py:16
  42.0 214.5 %collective-permute-start.2 = (bf16[2,256,512]{2,1,0:T(8,128)(2,1)}, bf16[2,256,512]{2,1,0:T(8,128)(2,1)}, u32[]{:S(2)}, u32[]{:S(2)}) collective-permute-start(bf16[2,256,512]{2,1,0:T(8,128)(2,1)} %pad_maximum_fusion), channel_id=1, source_target_pairs={{0,8},{4,12},{8,16},{12,20},{16,24},{20,28},{24,32},{28,36},{32,40... | collective-permute-start | bytes 1572872 | tf_op jit(solution)/shard_map/ppermute | solution.py:16
  44.2 218.5 %collective-permute-start.3 = (bf16[2,256,512]{2,1,0:T(8,128)(2,1)}, bf16[2,256,512]{2,1,0:T(8,128)(2,1)}, u32[]{:S(2)}, u32[]{:S(2)}) collective-permute-start(bf16[2,256,512]{2,1,0:T(8,128)(2,1)} %pad_maximum_fusion), channel_id=1, source_target_pairs={{0,4},{4,8},{8,12},{12,16},{16,20},{20,24},{24,28},{28,32},{32,36}... | collective-permute-start | bytes 1572872 | tf_op jit(solution)/shard_map/ppermute | solution.py:16
  46.1 217.7 %collective-permute-start.4 = (bf16[2,256,512]{2,1,0:T(8,128)(2,1)}, bf16[2,256,512]{2,1,0:T(8,128)(2,1)}, u32[]{:S(2)}, u32[]{:S(2)}) collective-permute-start(bf16[2,256,512]{2,1,0:T(8,128)(2,1)} %pad_maximum_fusion), channel_id=1, source_target_pairs={{4,0},{8,4},{12,8},{16,12},{20,16},{24,20},{28,24},{32,28},{36,32}... | collective-permute-start | bytes 1572872 | tf_op jit(solution)/shard_map/ppermute | solution.py:16
  54.1 209.7 %copy-start.5 = (bf16[1,256,512]{2,1,0:T(8,128)(2,1)S(1)}, bf16[1,256,512]{2,1,0:T(8,128)(2,1)}, u32[]{:S(2)}) copy-start(bf16[1,256,512]{2,1,0:T(8,128)(2,1)} %copy-done.4) | copy-start | bytes 786436
  228.3 36.6 %collective-permute-start.5 = (bf16[2,256,512]{2,1,0:T(8,128)(2,1)}, bf16[2,256,512]{2,1,0:T(8,128)(2,1)S(1)}, u32[]{:S(2)}, u32[]{:S(2)}) collective-permute-start(bf16[2,256,512]{2,1,0:T(8,128)(2,1)} %pad_maximum_fusion), channel_id=1, source_target_pairs={{8,0},{12,4},{16,8},{20,12},{24,16},{28,20},{32,24},{36,28},{40,32... | collective-permute-start | bytes 1572872 | tf_op jit(solution)/shard_map/ppermute | solution.py:16
  244.3 24.5 %collective-permute-start.6 = (bf16[2,256,512]{2,1,0:T(8,128)(2,1)}, bf16[2,256,512]{2,1,0:T(8,128)(2,1)S(1)}, u32[]{:S(2)}, u32[]{:S(2)}) collective-permute-start(bf16[2,256,512]{2,1,0:T(8,128)(2,1)} %pad_maximum_fusion), channel_id=1, source_target_pairs={{12,0},{16,4},{20,8},{24,12},{28,16},{32,20},{36,24},{40,28},{44,3... | collective-permute-start | bytes 1572872 | tf_op jit(solution)/shard_map/ppermute | solution.py:16
  256.6 34.4 %collective-permute-start.7 = (bf16[2,256,512]{2,1,0:T(8,128)(2,1)}, bf16[2,256,512]{2,1,0:T(8,128)(2,1)S(1)}, u32[]{:S(2)}, u32[]{:S(2)}) collective-permute-start(bf16[2,256,512]{2,1,0:T(8,128)(2,1)} %pad_maximum_fusion), channel_id=1, source_target_pairs={{16,0},{20,4},{24,8},{28,12},{32,16},{36,20},{40,24},{44,28},{48,3... | collective-permute-start | bytes 1572872 | tf_op jit(solution)/shard_map/ppermute | solution.py:16
  298.7 4.4 copy-start.12
  320.0 0.7 copy-start.7
  320.0 68.2 %copy-start.6 = (f32[2048]{0:T(1024)S(1)}, f32[2048]{0:T(1024)}, u32[]{:S(2)}) copy-start(f32[2048]{0:T(1024)} %param.17) | copy-start | bytes 24580
  320.1 269.3 %all-reduce.20.cloned.1.call-start = ((), (), s32[]{:S(2)}) async-start(), calls=%async_computation.2 | async-start | bytes 2097152 | tf_op jit(solution)/shard_map/pmax | solution.py:112
  386.2 2.2 copy-start.3
  400.1 272.9 %copy-start.1 = (bf16[512,2048]{1,0:T(8,128)(2,1)S(1)}, bf16[512,2048]{1,0:T(8,128)(2,1)}, u32[]{:S(2)}) copy-start(bf16[512,2048]{1,0:T(8,128)(2,1)} %param.15) | copy-start | bytes 6291460
  401.5 3.0 copy-start.9
  590.8 82.3 %copy-start.8 = (f32[128]{0:T(128)}, f32[128]{0:T(128)S(1)}, u32[]{:S(2)}) copy-start(f32[128]{0:T(128)S(1)} %get-tuple-element.7) | copy-start | bytes 1540
Sparse Core Ops, SparseCore 0:
  320.2 65.9 all-reduce.17
  404.0 185.3 all-reduce.19
